TPU v7x, 32 devices: a whole 2x2x4 slice. The times are simulated.
32 devices in a mesh: space: 8 (over z, x), fsdp: 4 (over y, core).
Axes of the slice: x: 2, y: 2, z: 4, core: 2. Of those that a mesh axis runs over, the one named last changes fastest.
Arguments:
- features: bfloat16 [4, 128, 8, 8, 512], P('fsdp', 'space'), may hold values from -6 to 6
- cotangent: bfloat16 [4, 128, 8, 8, 512], P('fsdp', 'space'), may hold values from -6 to 6
- tissue: int32 [4, 128], P('fsdp', 'space'), may hold values 0 or 1
- weight: bfloat16 [27, 64, 64], P(None, 'fsdp'), may hold values from -0.15625 to 0.15625
Outputs:
- activations: bfloat16 [4, 128, 8, 8, 512], P('fsdp', 'space')
- input_grad: bfloat16 [4, 128, 8, 8, 512], P('fsdp', 'space')
- weight_grad: float32 [27, 64, 64], P(None, 'fsdp')
All inputs are finite; a program needn't handle non-finite values. No bound on the sum of `tissue` on one device may be relied on, other than what follows from the above.
Results may differ from a plain program's by a relative error of at most 0.0034.
Values may be sent and summed in bfloat16 or wider, within the bound.
No kernel may reach another device: no remote copies, remote signals or barrier semaphores. Data moves between devices by JAX's collectives and lax.ppermute only.
A program may use at most 192 MiB of HBM per device.

v0:
```python
import math
import jax
import jax.numpy as jnp
from jax import lax
from jax.sharding import PartitionSpec as P

BRICK_X = 2
BRICK_Y = 2
BRICK_Z = 4
PAIR = 2
DEPTH = 2
CONV_DIMS = ("NDHWC", "DHWIO", "NDHWC")


def from_behind(shard, axis, by):
    peers = lax.axis_size(axis)
    pairs = [(i, i + by) for i in range(peers) if 0 <= i + by < peers]
    return lax.ppermute(shard, axis, pairs)


def grid_shape(number):
    factors = [1, 1, 1]
    places = 0
    while number % 2 == 0:
        factors[places % 3] = factors[places % 3] * 2
        number = number // 2
        places = places + 1
    factors[0] = factors[0] * number
    return factors


def to_volume(bricks, edge_cells, lanes):
    per_brick = edge_cells // PAIR
    blocks = bricks.reshape(BRICK_X, BRICK_Y, BRICK_Z, edge_cells, edge_cells, per_brick, lanes)
    blocks = blocks.transpose(0, 3, 1, 4, 2, 5, 6)
    return blocks.reshape(BRICK_X * edge_cells, BRICK_Y * edge_cells, BRICK_Z * per_brick, lanes)


def to_bricks(volume, edge_cells, lanes):
    per_brick = edge_cells // PAIR
    blocks = volume.reshape(BRICK_X, edge_cells, BRICK_Y, edge_cells, BRICK_Z, per_brick, lanes)
    blocks = blocks.transpose(0, 2, 4, 1, 3, 5, 6)
    return blocks.reshape(BRICK_X * BRICK_Y * BRICK_Z, edge_cells, edge_cells, per_brick * lanes)


def neighbour_plane(portion, offset, present):
    arrived = from_behind(portion, "space", offset)
    return jnp.where(present, arrived, jnp.zeros_like(arrived))


def extend(volume, grid_dims, places, widths):
    strides = (grid_dims[1] * grid_dims[2], grid_dims[2], 1)
    for axis_pos in range(3):
        axis = axis_pos + 1
        extent = volume.shape[axis]
        width = widths[axis_pos]
        last_layer = lax.slice_in_dim(volume, extent - width, extent, axis=axis)
        first_layer = lax.slice_in_dim(volume, 0, width, axis=axis)
        from_below = neighbour_plane(last_layer, strides[axis_pos], places[axis_pos] > 0)
        from_above = neighbour_plane(
            first_layer, -strides[axis_pos], places[axis_pos] < grid_dims[axis_pos] - 1
        )
        volume = jnp.concatenate([from_below, volume, from_above], axis=axis)
    return volume


def super_kernel(weight_full, channels):
    taps = weight_full.reshape(3, 3, 3, channels, channels)
    zero = jnp.zeros((3, 3, channels, channels), weight_full.dtype)
    rows = []
    for dz in range(3):
        row = []
        for hi in range(PAIR):
            col = []
            for ho in range(PAIR):
                c = 2 * dz - 1 + hi - ho
                col.append(taps[:, :, c] if 0 <= c < 3 else zero)
            row.append(jnp.concatenate(col, axis=-1))
        rows.append(jnp.concatenate(row, axis=-2))
    return jnp.stack(rows, axis=2)


def fold_kernel_grad(grad_sup, channels):
    taps = [None, None, None]
    for dz in range(3):
        for hi in range(PAIR):
            for ho in range(PAIR):
                c = 2 * dz - 1 + hi - ho
                if 0 <= c < 3:
                    block = grad_sup[
                        :,
                        :,
                        dz,
                        hi * channels : (hi + 1) * channels,
                        ho * channels : (ho + 1) * channels,
                    ]
                    taps[c] = block if taps[c] is None else taps[c] + block
    return jnp.stack(taps, axis=2).reshape(27, channels, channels)


def conv(volume, kernel):
    return lax.conv_general_dilated(
        volume[None],
        kernel,
        (1, 1, 1),
        "VALID",
        dimension_numbers=CONV_DIMS,
        preferred_element_type=jnp.float32,
    )[0]


def kernel_grad(inputs, grads):
    out = lax.conv_general_dilated(
        inputs[None],
        grads[None],
        (1, 1, 1),
        "VALID",
        dimension_numbers=("CDHWN", "IDHWO", "NDHWC"),
        preferred_element_type=jnp.float32,
    )
    return out.transpose(1, 2, 3, 0, 4)


def local(features, cotangent, tissue, weight):
    edge_cells = features.shape[2]
    channels = weight.shape[2]
    lanes = PAIR * channels
    grid_dims = grid_shape(lax.axis_size("space"))
    index_now = lax.axis_index("space")
    places = (
        index_now // (grid_dims[1] * grid_dims[2]),
        index_now // grid_dims[2] % grid_dims[1],
        index_now % grid_dims[2],
    )
    weight_full = lax.all_gather(weight, "fsdp", axis=1, tiled=True)
    k_fwd = super_kernel(weight_full, channels)
    k_back = jnp.flip(k_fwd, (0, 1, 2)).transpose(0, 1, 2, 4, 3)
    present = tissue[0][:, None, None, None] > 0
    inputs = features[0]
    incoming = cotangent[0]
    masked = jnp.where(present, inputs, jnp.zeros_like(inputs))
    masked_cot = jnp.where(present, incoming, jnp.zeros_like(incoming))
    both = jnp.stack(
        [to_volume(masked, edge_cells, lanes), to_volume(masked_cot, edge_cells, lanes)]
    )
    grown = extend(both, grid_dims, places, (DEPTH, DEPTH, 1))
    grown = jnp.pad(grown, ((0, 0), (0, 0), (0, 0), (1, 1), (0, 0)))
    padded_in = grown[0]
    cot_ext = grown[1, 1:-1, 1:-1, 1:-1]
    pre_ext = conv(padded_in, k_fwd)
    gate_ext = jax.nn.sigmoid(pre_ext)
    slope_ext = gate_ext * (1.0 + pre_ext * (1.0 - gate_ext))
    grad_ext = (cot_ext.astype(jnp.float32) * slope_ext).astype(jnp.bfloat16)
    tissue_mask = tissue[0].astype(jnp.float32)[:, None, None, None]
    pre = to_bricks(pre_ext[1:-1, 1:-1, 1:-1], edge_cells, lanes)
    gate_val = to_bricks(gate_ext[1:-1, 1:-1, 1:-1], edge_cells, lanes)
    activations = (tissue_mask * (inputs.astype(jnp.float32) + pre * gate_val)).astype(jnp.bfloat16)
    back = to_bricks(conv(grad_ext, k_back), edge_cells, lanes)
    input_grad = (tissue_mask * (incoming.astype(jnp.float32) + back)).astype(jnp.bfloat16)
    total_cells = (
        lax.axis_size("space") * lax.axis_size("fsdp") * BRICK_X * BRICK_Y * BRICK_Z * edge_cells**3
    )
    grad_sup = kernel_grad(padded_in[1:-1, 1:-1, 1:-1], grad_ext[1:-1, 1:-1, 1:-1])
    grad_term = fold_kernel_grad(grad_sup, channels) / math.sqrt(total_cells)
    grad_part = lax.psum_scatter(grad_term, "fsdp", scatter_dimension=1, tiled=True)
    grad_part = lax.psum(grad_part, "space")
    return (activations[None], input_grad[None], grad_part)


def solution(mesh):
    return jax.shard_map(
        local,
        mesh=mesh,
        in_specs=(
            P("fsdp", "space", None, None, None),
            P("fsdp", "space", None, None, None),
            P("fsdp", "space"),
            P(None, "fsdp", None),
        ),
        out_specs=(
            P("fsdp", "space", None, None, None),
            P("fsdp", "space", None, None, None),
            P(None, "fsdp", None),
        ),
        check_vma=False,
    )
```

profile of v0, /device:TPU:0, one launch (start us, length us, event | category | flops | bytes accessed | tf_op | source)
XLA Modules:
  0.0 291.2 jit_solution(907447351510930595)
XLA Ops:
  7.2 0.7 compare_reduce_fusion
  8.0 2.7 copy_select_fusion.1
  10.7 1.3 collective-permute-start.1
  12.0 6.7 %collective-permute-start = (bf16[2,2,16,16,128]{4,3,2,1,0:T(8,128)(2,1)S(1)}, bf16[2,2,16,16,128]{4,3,2,1,0:T(8,128)(2,1)S(1)}, u32[]{:S(2)}, u32[]{:S(2)}) collective-permute-start(bf16[2,2,16,16,128]{4,3,2,1,0:T(8,128)(2,1)S(1)} %get-tuple-element.11), channel_id=1, source_target_pairs={{0,16},{4,20},{8,24},{12,28},{1,17},{5,21},{9,25},{13,29},{2,18},{... | collective-permute-start | bytes 786440 | tf_op jit(solution)/shard_map/ppermute | solution.py:18
  18.7 7.7 %all_gather.3 = bf16[27,64,64]{2,1,0:T(8,128)(2,1)S(1)} all-gather(bf16[27,16,64]{2,1,0:T(8,128)(2,1)S(1)} %copy-done.14), channel_id=1, replica_groups=mesh['space'=8,'fsdp'=4] {'fsdp'}, dimensions={1}, use_global_device_ids=true | all-gather | bytes 276480 | tf_op jit(solution)/shard_map/all_gather | solution.py:135
  26.4 1.7 collective-permute-done.1
  28.1 1.0 broadcast_select_fusion.5
  29.2 1.3 collective-permute-start.3
  30.6 4.8 %collective-permute-start.2 = (bf16[2,20,2,16,128]{4,3,2,1,0:T(8,128)(2,1)S(1)}, bf16[2,20,2,16,128]{4,3,2,1,0:T(8,128)(2,1)S(1)}, u32[]{:S(2)}, u32[]{:S(2)}) collective-permute-start(bf16[2,20,2,16,128]{4,3,2,1,0:T(8,128)(2,1)S(1)} %get-tuple-element.9), channel_id=1, source_target_pairs={{0,8},{4,12},{8,16},{12,20},{16,24},{20,28},{1,9},{5,13},{9,17},{1... | collective-permute-start | bytes 983048 | tf_op jit(solution)/shard_map/ppermute | solution.py:18
  35.7 5.6 %collective-permute-done.3 = bf16[2,20,2,16,128]{4,3,2,1,0:T(8,128)(2,1)S(1)} collective-permute-done((bf16[2,20,2,16,128]{4,3,2,1,0:T(8,128)(2,1)S(1)}, bf16[2,20,2,16,128]{4,3,2,1,0:T(8,128)(2,1)S(1)}, u32[]{:S(2)}, u32[]{:S(2)}) %collective-permute-start.3) | collective-permute-done | bytes 327712 | tf_op jit(solution)/shard_map/ppermute | solution.py:18
  41.3 1.2 collective-permute-done.2
  42.5 1.9 pad_maximum_fusion.7
  44.4 1.3 collective-permute-start.5
  45.7 0.5 convert_bitcast_fusion.1
  46.2 4.7 %collective-permute-start.4 = (bf16[2,20,20,1,128]{4,3,2,1,0:T(2,128)(2,1)S(1)}, bf16[2,20,20,1,128]{4,3,2,1,0:T(2,128)(2,1)S(1)}, u32[]{:S(2)}, u32[]{:S(2)}) collective-permute-start(bf16[2,20,20,1,128]{4,3,2,1,0:T(2,128)(2,1)S(1)} %get-tuple-element.7), channel_id=1, source_target_pairs={{0,4},{4,8},{8,12},{12,16},{16,20},{20,24},{24,28},{1,5},{5,9},{9,... | collective-permute-start | bytes 614408 | tf_op jit(solution)/shard_map/ppermute | solution.py:18
  50.9 6.3 %collective-permute-done.5 = bf16[2,20,20,1,128]{4,3,2,1,0:T(2,128)(2,1)S(1)} collective-permute-done((bf16[2,20,20,1,128]{4,3,2,1,0:T(2,128)(2,1)S(1)}, bf16[2,20,20,1,128]{4,3,2,1,0:T(2,128)(2,1)S(1)}, u32[]{:S(2)}, u32[]{:S(2)}) %collective-permute-start.5) | collective-permute-done | bytes 204832 | tf_op jit(solution)/shard_map/ppermute | solution.py:18
  57.2 0.4 broadcast_select_fusion.1
  57.7 8.5 %collective-permute-done.4 = bf16[2,20,20,1,128]{4,3,2,1,0:T(2,128)(2,1)S(1)} collective-permute-done((bf16[2,20,20,1,128]{4,3,2,1,0:T(2,128)(2,1)S(1)}, bf16[2,20,20,1,128]{4,3,2,1,0:T(2,128)(2,1)S(1)}, u32[]{:S(2)}, u32[]{:S(2)}) %collective-permute-start.4) | collective-permute-done | bytes 204832 | tf_op jit(solution)/shard_map/ppermute | solution.py:18
  66.6 5.9 %pad_maximum_fusion = bf16[2,20,20,18,128]{4,3,2,1,0:T(8,128)(2,1)S(1)} fusion(bf16[2,20,20,1,128]{4,3,2,1,0:T(2,128)(2,1)S(1)} %broadcast_select_fusion.1, bf16[2,20,2,16,128]{4,3,2,1,0:T(8,128)(2,1)S(1)} %broadcast_select_fusion.3, bf16[2,2,16,16,128]{4,3,2,1,0:T(8,128)(2,1)S(1)} %broadcast_select_fusion.5, bf16[1,16,16,16,128]{4,3,2,1,0:T(8,128)(2,1)S(1)} %bitcast.89, ...), kind=kLoop, calls=%fused_computation.6 | loop fusion | flops 29491200 | bytes 7372800 | tf_op jit(solution)/shard_map/concatenate | solution.py:63
  72.5 3.0 %fusion.29 = (bf16[20,20,20,128]{3,2,1,0:T(8,128)(2,1)}, bf16[20,20,1,20,128]{4,3,1,0,2:T(8,128)(2,1)S(1)}) fusion(bf16[2,20,20,18,128]{4,3,2,1,0:T(8,128)(2,1)S(1)} %pad_maximum_fusion), kind=kLoop, calls=%fused_computation.39 | loop fusion | bytes 7782400 | tf_op jit(solution)/shard_map/squeeze | solution.py:148
  75.8 0.7 pad.9.clone
  76.9 0.5 slice.93
  77.5 17.0 %add_multiply_fusion = (f32[18,18,8,3,128]{4,2,3,1,0:T(8,128)}, f32[18,18,8,3,128]{4,2,3,1,0:T(8,128)S(1)}) fusion(bf16[3,3,1,128,128]{4,3,2,1,0:T(8,128)(2,1)S(1)} %get-tuple-element.21, bf16[3,3,1,128,128]{4,3,2,1,0:T(8,128)(2,1)S(1)} %get-tuple-element.20, bf16[3,3,1,128,128]{4,3,2,1,0:T(8,128)(2,1)S(1)} %get-tuple-element.19, ...), kind=kOutput, calls=%fused_computation.17 | convolution fusion | flops 6900842496 | bytes 12738584 | tf_op jit(solution)/shard_map/conv_general_dilated | solution.py:102
  94.4 4.0 %copy.40 = f32[18,18,8,3,128]{4,3,2,1,0:T(4,128)} copy(f32[18,18,8,3,128]{4,2,3,1,0:T(8,128)S(1)} %get-tuple-element.27) | data formatting | bytes 7962624 | tf_op jit(solution)/shard_map/conv_general_dilated | solution.py:102
  98.4 7.3 %reshape.72 = f32[18,18,1,24,128]{4,3,1,0,2:T(8,128)} reshape(f32[18,18,8,3,128]{4,3,2,1,0:T(4,128)} %copy.40) | data formatting | bytes 7962624 | tf_op jit(solution)/shard_map/conv_general_dilated | solution.py:102
  105.7 4.5 %slice_bitcast_fusion.1 = f32[18,18,18,128]{3,2,1,0:T(8,128)} fusion(f32[18,18,1,24,128]{4,3,1,0,2:T(8,128)} %reshape.72), kind=kLoop, calls=%fused_computation.16 | loop fusion | bytes 5971968 | tf_op jit(solution)/shard_map/squeeze | solution.py:102
  110.2 3.0 %add_divide_fusion = f32[18,18,18,128]{3,2,1,0:T(8,128)} fusion(f32[18,18,1,24,128]{4,3,1,0,2:T(8,128)S(1)} %copy-done.1), kind=kLoop, calls=%fused_computation.18 | loop fusion | flops 2239488 | bytes 5971968 | tf_op jit(solution)/shard_map/div | solution.py:151
  113.2 3.9 %convert_bitcast_fusion = f32[18,18,18,128]{3,2,1,0:T(8,128)} fusion(bf16[2,20,20,18,128]{4,3,2,1,0:T(8,128)(2,1)} %copy-done), kind=kLoop, calls=%fused_computation.4 | loop fusion | flops 746496 | bytes 4478976 | tf_op jit(solution)/shard_map/convert_element_type | solution.py:153
  117.1 4.0 %copy.42 = f32[18,18,8,3,128]{4,3,2,1,0:T(4,128)} copy(f32[18,18,8,3,128]{4,2,3,1,0:T(8,128)S(1)} %copy-done.9) | data formatting | bytes 7962624 | tf_op jit(solution)/shard_map/mul | solution.py:152
  121.0 7.3 %reshape.81 = f32[18,18,1,24,128]{4,3,1,0,2:T(8,128)} reshape(f32[18,18,8,3,128]{4,3,2,1,0:T(4,128)} %copy.42) | data formatting | bytes 7962624 | tf_op jit(solution)/shard_map/mul | solution.py:152
  128.3 3.2 %fusion.22 = bf16[18,18,1,18,128]{4,3,1,0,2:T(8,128)(2,1)S(1)} fusion(f32[18,18,1,24,128]{4,3,1,0,2:T(8,128)} %reshape.81, bf16[2,20,20,18,128]{4,3,2,1,0:T(8,128)(2,1)} %copy-done), kind=kLoop, calls=%fused_computation.33 | loop fusion | flops 2239488 | bytes 5971968 | tf_op jit(solution)/shard_map/convert_element_type | solution.py:153
  131.5 1.6 pad.11
  133.1 5.5 %reshape.75 = bf16[18,18,1,8,3,128]{5,4,3,1,0,2:T(4,128)(2,1)S(1)} reshape(bf16[18,18,1,24,128]{4,3,1,0,2:T(8,128)(2,1)} %pad.11) | data formatting | bytes 3981312 | tf_op jit(solution)/shard_map/conv_general_dilated | solution.py:102
  139.1 1.3 copy-done.6
  140.3 1.5 slice.102
  141.9 1.1 slice_bitcast_fusion.2
  143.0 1.2 copy-done.2
  144.1 4.3 %fusion.31 = (bf16[1,16,16,16,128]{4,3,2,1,0:T(8,128)(2,1)S(1)}, f32[16,16,16,128]{3,2,1,0:T(8,128)}) fusion(f32[18,18,18,128]{3,2,1,0:T(8,128)S(1)} %copy-done.2, f32[18,18,18,128]{3,2,1,0:T(8,128)S(1)} %copy-done.3, f32[18,18,18,128]{3,2,1,0:T(8,128)} %convert_bitcast_fusion), kind=kLoop, calls=%fused_computation.41 | loop fusion | flops 3670016 | bytes 9437184 | tf_op jit(solution)/shard_map/broadcast_in_dim | solution.py:115
  148.4 32.2 %fusion.17 = f32[3,3,3,128,128]{4,3,2,1,0:T(8,128)S(1)} fusion(bf16[1,18,18,18,128]{4,3,2,1,0:T(8,128)(2,1)S(1)} %slice_bitcast_fusion.2, bf16[1,16,16,16,128]{4,3,2,1,0:T(8,128)(2,1)S(1)} %get-tuple-element.3), kind=kOutput, calls=%fused_computation.25 | convolution fusion | flops 3623878656 | bytes 4311040 | tf_op jit(solution)/shard_map/transpose | solution.py:121
  181.0 1.0 maximum_multiply_fusion
  182.9 13.3 %fusion.25 = f32[16,16,8,3,128]{4,2,3,1,0:T(8,128)S(1)} fusion(bf16[18,18,1,7,2,128]{5,3,4,1,0,2:T(8,128)(2,1)S(1)} %copy-done.10, bf16[18,18,1,8,3,128]{5,3,4,1,0,2:T(8,128)(2,1)S(1)} %copy-done.7, pred[8,3]{0,1:T(4,128)(4,1)S(1)} %copy-done.17, bf16[3,3,1,128,128]{4,3,2,1,0:T(8,128)(2,1)} %copy-done.13, bf16[3,3,1,128,128]{4,3,2,1,0:T(8,128)(2,1)} %copy-done.12, ...), kind=kOutput, calls=%fused_computation.37 | convolution fusion | flops 5447442432 | bytes 7182360 | tf_op jit(solution)/shard_map/conv_general_dilated | solution.py:102
  196.3 0.5 copy.45
  197.3 1.1 copy-done.4
  198.4 2.0 copy.41
  200.4 7.6 %reduce-scatter.2.cloned.1.call-done = f32[27,16,64]{2,1,0:T(8,128)} async-done(((f32[27,64,64]{2,1,0:T(8,128)}), f32[27,16,64]{2,1,0:T(8,128)}) %reduce-scatter.2.cloned.1.call-update) | async-done | bytes 110608 | tf_op jit(solution)/shard_map/reduce_scatter | solution.py:165
  208.1 4.2 %multiply_convert_fusion = (bf16[1,16,8,8,512]{4,3,2,1,0:T(8,128)(2,1)}, bf16[1,16,8,8,512]{4,3,2,1,0:T(8,128)(2,1)}) fusion(f32[1,16,8,8,512]{4,3,2,1,0:T(8,128)S(1)} %bitcast.94, bf16[1,16,8,8,512]{4,3,2,1,0:T(8,128)(2,1)} %param.5, f32[16]{0:T(128)S(1)} %copy-done.15, f32[1,16,8,8,512]{4,3,2,1,0:T(8,128)} %bitcast.95, ...), kind=kLoop, calls=%fused_computation.29 | loop fusion | flops 4194304 | bytes 8388672 | tf_op jit(solution)/shard_map/convert_element_type | solution.py:159
  212.3 70.0 %all-reduce.7.cloned.1.call-done = f32[27,16,64]{2,1,0:T(8,128)} async-done(((f32[27,16,64]{2,1,0:T(8,128)}), f32[27,16,64]{2,1,0:T(8,128)}) %all-reduce.7.cloned.1.call-update) | async-done | bytes 110608 | tf_op jit(solution)/shard_map/psum | solution.py:166
  282.2 1.6 copy.60
  (55 shorter events, 3.9 us)
Async XLA Ops:
  7.2 11.5 %copy-start.14 = (bf16[27,16,64]{2,1,0:T(8,128)(2,1)S(1)}, bf16[27,16,64]{2,1,0:T(8,128)(2,1)}, u32[]{:S(2)}) copy-start(bf16[27,16,64]{2,1,0:T(8,128)(2,1)} %param.7) | copy-start | bytes 165892
  7.2 200.8 %reduce-scatter.2.cloned.1.call-start = ((), (), s32[]{:S(2)}) async-start(), calls=%async_computation.1 | async-start | bytes 1105920 | tf_op jit(solution)/shard_map/reduce_scatter | solution.py:165
  10.7 17.4 %collective-permute-start.1 = (bf16[2,2,16,16,128]{4,3,2,1,0:T(8,128)(2,1)S(1)}, bf16[2,2,16,16,128]{4,3,2,1,0:T(8,128)(2,1)}, u32[]{:S(2)}, u32[]{:S(2)}) collective-permute-start(bf16[2,2,16,16,128]{4,3,2,1,0:T(8,128)(2,1)S(1)} %get-tuple-element.12), channel_id=1, source_target_pairs={{16,0},{20,4},{24,8},{28,12},{17,1},{21,5},{25,9},{29,13},{18,2},{... | collective-permute-start | bytes 786440 | tf_op jit(solution)/shard_map/ppermute | solution.py:18
  12.0 17.0 %collective-permute-start = (bf16[2,2,16,16,128]{4,3,2,1,0:T(8,128)(2,1)S(1)}, bf16[2,2,16,16,128]{4,3,2,1,0:T(8,128)(2,1)S(1)}, u32[]{:S(2)}, u32[]{:S(2)}) collective-permute-start(bf16[2,2,16,16,128]{4,3,2,1,0:T(8,128)(2,1)S(1)} %get-tuple-element.11), channel_id=1, source_target_pairs={{0,16},{4,20},{8,24},{12,28},{1,17},{5,21},{9,25},{13,29},{2,18},{... | collective-permute-start | bytes 786440 | tf_op jit(solution)/shard_map/ppermute | solution.py:18
  29.2 16.5 %copy-start.16 = (s32[1,16]{1,0:T(1,128)S(1)}, s32[1,16]{1,0:T(1,128)}, u32[]{:S(2)}) copy-start(s32[1,16]{1,0:T(1,128)} %param.6) | copy-start | bytes 196
  29.2 12.0 %collective-permute-start.3 = (bf16[2,20,2,16,128]{4,3,2,1,0:T(8,128)(2,1)S(1)}, bf16[2,20,2,16,128]{4,3,2,1,0:T(8,128)(2,1)S(1)}, u32[]{:S(2)}, u32[]{:S(2)}) collective-permute-start(bf16[2,20,2,16,128]{4,3,2,1,0:T(8,128)(2,1)S(1)} %get-tuple-element.10), channel_id=1, source_target_pairs={{8,0},{12,4},{16,8},{20,12},{24,16},{28,20},{9,1},{13,5},{17,9},{2... | collective-permute-start | bytes 983048 | tf_op jit(solution)/shard_map/ppermute | solution.py:18
  30.6 11.9 %collective-permute-start.2 = (bf16[2,20,2,16,128]{4,3,2,1,0:T(8,128)(2,1)S(1)}, bf16[2,20,2,16,128]{4,3,2,1,0:T(8,128)(2,1)S(1)}, u32[]{:S(2)}, u32[]{:S(2)}) collective-permute-start(bf16[2,20,2,16,128]{4,3,2,1,0:T(8,128)(2,1)S(1)} %get-tuple-element.9), channel_id=1, source_target_pairs={{0,8},{4,12},{8,16},{12,20},{16,24},{20,28},{1,9},{5,13},{9,17},{1... | collective-permute-start | bytes 983048 | tf_op jit(solution)/shard_map/ppermute | solution.py:18
  35.6 41.8 %copy-start.11 = (bf16[3,3,1,128,128]{4,3,2,1,0:T(8,128)(2,1)}, bf16[3,3,1,128,128]{4,3,2,1,0:T(8,128)(2,1)S(1)}, u32[]{:S(2)}) copy-start(bf16[3,3,1,128,128]{4,3,2,1,0:T(8,128)(2,1)S(1)} %get-tuple-element.19) | copy-start | bytes 884740
  35.6 41.8 %copy-start.12 = (bf16[3,3,1,128,128]{4,3,2,1,0:T(8,128)(2,1)}, bf16[3,3,1,128,128]{4,3,2,1,0:T(8,128)(2,1)S(1)}, u32[]{:S(2)}) copy-start(bf16[3,3,1,128,128]{4,3,2,1,0:T(8,128)(2,1)S(1)} %get-tuple-element.20) | copy-start | bytes 884740
  35.6 41.8 %copy-start.13 = (bf16[3,3,1,128,128]{4,3,2,1,0:T(8,128)(2,1)}, bf16[3,3,1,128,128]{4,3,2,1,0:T(8,128)(2,1)S(1)}, u32[]{:S(2)}) copy-start(bf16[3,3,1,128,128]{4,3,2,1,0:T(8,128)(2,1)S(1)} %get-tuple-element.21) | copy-start | bytes 884740
  44.4 12.9 %collective-permute-start.5 = (bf16[2,20,20,1,128]{4,3,2,1,0:T(2,128)(2,1)S(1)}, bf16[2,20,20,1,128]{4,3,2,1,0:T(2,128)(2,1)S(1)}, u32[]{:S(2)}, u32[]{:S(2)}) collective-permute-start(bf16[2,20,20,1,128]{4,3,2,1,0:T(2,128)(2,1)S(1)} %get-tuple-element.8), channel_id=1, source_target_pairs={{4,0},{8,4},{12,8},{16,12},{20,16},{24,20},{28,24},{5,1},{9,5},{13... | collective-permute-start | bytes 614408 | tf_op jit(solution)/shard_map/ppermute | solution.py:18
  46.2 20.0 %collective-permute-start.4 = (bf16[2,20,20,1,128]{4,3,2,1,0:T(2,128)(2,1)S(1)}, bf16[2,20,20,1,128]{4,3,2,1,0:T(2,128)(2,1)S(1)}, u32[]{:S(2)}, u32[]{:S(2)}) collective-permute-start(bf16[2,20,20,1,128]{4,3,2,1,0:T(2,128)(2,1)S(1)} %get-tuple-element.7), channel_id=1, source_target_pairs={{0,4},{4,8},{8,12},{12,16},{16,20},{20,24},{24,28},{1,5},{5,9},{9,... | collective-permute-start | bytes 614408 | tf_op jit(solution)/shard_map/ppermute | solution.py:18
  72.5 3.0 %copy-start = (bf16[2,20,20,18,128]{4,3,2,1,0:T(8,128)(2,1)}, bf16[2,20,20,18,128]{4,3,2,1,0:T(8,128)(2,1)S(1)}, u32[]{:S(2)}) copy-start(bf16[2,20,20,18,128]{4,3,2,1,0:T(8,128)(2,1)S(1)} %pad_maximum_fusion) | copy-start | bytes 11059204
  76.6 0.8 copy-start.18
  105.7 4.5 %copy-start.1 = (f32[18,18,1,24,128]{4,3,1,0,2:T(8,128)S(1)}, f32[18,18,1,24,128]{4,3,1,0,2:T(8,128)}, u32[]{:S(2)}) copy-start(f32[18,18,1,24,128]{4,3,1,0,2:T(8,128)} %reshape.72) | copy-start | bytes 11943940
  113.2 3.9 %copy-start.9 = (f32[18,18,8,3,128]{4,2,3,1,0:T(8,128)S(1)}, f32[18,18,8,3,128]{4,2,3,1,0:T(8,128)}, u32[]{:S(2)}) copy-start(f32[18,18,8,3,128]{4,2,3,1,0:T(8,128)} %get-tuple-element.26) | copy-start | bytes 11943940
  138.7 3.2 %copy-start.5 = (bf16[20,20,20,128]{3,2,1,0:T(8,128)(2,1)S(1)}, bf16[20,20,20,128]{3,2,1,0:T(8,128)(2,1)}, u32[]{:S(2)}) copy-start(bf16[20,20,20,128]{3,2,1,0:T(8,128)(2,1)} %get-tuple-element.5) | copy-start | bytes 6144004
  138.7 4.3 %copy-start.3 = (f32[18,18,18,128]{3,2,1,0:T(8,128)S(1)}, f32[18,18,18,128]{3,2,1,0:T(8,128)}, u32[]{:S(2)}) copy-start(f32[18,18,18,128]{3,2,1,0:T(8,128)} %add_divide_fusion) | copy-start | bytes 8957956
  139.1 1.3 copy-start.6
  140.3 3.8 %copy-start.2 = (f32[18,18,18,128]{3,2,1,0:T(8,128)S(1)}, f32[18,18,18,128]{3,2,1,0:T(8,128)}, u32[]{:S(2)}) copy-start(f32[18,18,18,128]{3,2,1,0:T(8,128)} %slice_bitcast_fusion.1) | copy-start | bytes 8957956
  180.7 1.9 copy-start.7
  180.7 2.2 copy-start.10
  180.7 2.2 copy-start.17
  182.0 100.2 %all-reduce.7.cloned.1.call-start = ((), (), s32[]{:S(2)}) async-start(), calls=%async_computation.2 | async-start | bytes 442368 | tf_op jit(solution)/shard_map/psum | solution.py:166
  196.8 1.6 copy-start.4
  197.0 11.1 %copy-start.8 = (bf16[1,16,8,8,512]{4,3,2,1,0:T(8,128)(2,1)S(1)}, bf16[1,16,8,8,512]{4,3,2,1,0:T(8,128)(2,1)}, u32[]{:S(2)}) copy-start(bf16[1,16,8,8,512]{4,3,2,1,0:T(8,128)(2,1)} %param.4) | copy-start | bytes 3145732
  197.0 11.1 %copy-start.15 = (f32[16]{0:T(128)S(1)}, f32[16]{0:T(128)}, u32[]{:S(2)}) copy-start(f32[16]{0:T(128)} %convert_bitcast_fusion.1) | copy-start | bytes 196
Sparse Core Ops, SparseCore 0:
  182.2 25.7 reduce-scatter.1
  211.4 70.8 all-reduce.6
where the time goes:
time: 296 us; the launch traced here: 291 us
  waiting for transfers between devices  101 us (34%)
  matrix products  62.5 us (21%)
  local copies, waits for them, and re-layouts  51 us (17%)
  other arithmetic  33.8 us (11%)
  starting transfers between devices  20.3 us (7%)
  between operations  14.9 us (5%)
  blocking collectives  7.7 us (3%)
    psum x1, waiting for transfers between devices, local(): grad_part = lax.psum(grad_part, 'space')  70 us
    transpose x1, matrix products, kernel_grad(): return out.transpose(1, 2, 3, 0, 4)  32.2 us
    conv_general_dilated x2, matrix products, conv(): lax.conv_general_dilated(volume[None], kernel, (1, 1, 1), 'VALID', dimens...  30.3 us
    ppermute x6, waiting for transfers between devices, from_behind(): return lax.ppermute(shard, axis, pairs)  23.2 us
    conv_general_dilated x9, local copies, waits for them, and re-layouts, conv(): lax.conv_general_dilated(volume[None], kernel, (1, 1, 1), 'VALID', dimens...  20.1 us
    ppermute x6, starting transfers between devices, from_behind(): return lax.ppermute(shard, axis, pairs)  20 us
    mul x2, local copies, waits for them, and re-layouts, local(): slope_ext = gate_ext * (1.0 + pre_ext * (1.0 - gate_ext))  11.3 us
    all_gather x1, blocking collectives, local(): weight_full = lax.all_gather(weight, 'fsdp', axis=1, tiled=True)  7.7 us
  transfers between devices with their start and end apart: 8, of which 7 were waited for; matrix products, arithmetic and copies ran while one was open for 8% of the time, Pallas kernels for 0%

commit v1 on v0

--- a/solution.py
+++ b/solution.py
@@ -163,7 +163,7 @@
     grad_sup = kernel_grad(padded_in[1:-1, 1:-1, 1:-1], grad_ext[1:-1, 1:-1, 1:-1])
     grad_term = fold_kernel_grad(grad_sup, channels) / math.sqrt(total_cells)
     grad_part = lax.psum_scatter(grad_term, "fsdp", scatter_dimension=1, tiled=True)
-    grad_part = lax.psum(grad_part, "space")
+    grad_part = jnp.sum(lax.all_gather(grad_part, "space"), axis=0)
     return (activations[None], input_grad[None], grad_part)
 
 

time: 296 us -> 257 us (0.87)
  waiting for transfers between devices: 101 us -> 29.6 us
  blocking collectives: 7.7 us -> 47.2 us
  local copies, waits for them, and re-layouts: 51 us -> 45.1 us
    psum x1 -> x0, waiting for transfers between devices: 70 us -> none  [local(): grad_part = lax.psum(grad_part, 'space')]
    all_gather x0 -> x1, blocking collectives: none -> 39.5 us  [local(): grad_part = jnp.sum(lax.all_gather(grad_part, 'space'), axis=0)]
    unnamed x40 -> x41, local copies, waits for them, and re-layouts: 6.21 us -> 3.55 us
  transfers between devices with their start and end apart: 8 -> 7, of which waited for: 7 -> 6; matrix products, arithmetic and copies ran while one was open for 8% -> 8% of each run, Pallas kernels for 0% -> 0%
where the time goes in v1:
time: 257 us; the launch traced here: 253 us
  matrix products  63 us (25%)
  blocking collectives  47.2 us (18%)
  local copies, waits for them, and re-layouts  45.1 us (18%)
  other arithmetic  32.7 us (13%)
  waiting for transfers between devices  29.6 us (12%)
  starting transfers between devices  20.1 us (8%)
  between operations  14.9 us (6%)
    all_gather x1, blocking collectives, local(): grad_part = jnp.sum(lax.all_gather(grad_part, 'space'), axis=0)  39.5 us
    transpose x1, matrix products, kernel_grad(): return out.transpose(1, 2, 3, 0, 4)  32.2 us
    conv_general_dilated x2, matrix products, conv(): lax.conv_general_dilated(volume[None], kernel, (1, 1, 1), 'VALID', dimens...  30.8 us
    ppermute x6, waiting for transfers between devices, from_behind(): return lax.ppermute(shard, axis, pairs)  23.2 us
    ppermute x6, starting transfers between devices, from_behind(): return lax.ppermute(shard, axis, pairs)  20 us
    conv_general_dilated x9, local copies, waits for them, and re-layouts, conv(): lax.conv_general_dilated(volume[None], kernel, (1, 1, 1), 'VALID', dimens...  19.5 us
    mul x2, local copies, waits for them, and re-layouts, local(): slope_ext = gate_ext * (1.0 + pre_ext * (1.0 - gate_ext))  11.3 us
    all_gather x1, blocking collectives, local(): weight_full = lax.all_gather(weight, 'fsdp', axis=1, tiled=True)  7.7 us
  transfers between devices with their start and end apart: 7, of which 6 were waited for; matrix products, arithmetic and copies ran while one was open for 8% of the time, Pallas kernels for 0%

profile of v1, /device:TPU:0, one launch (start us, length us, event | category | flops | bytes accessed | tf_op | source)
XLA Modules:
  0.0 252.6 jit_solution(14823312713849300885)
XLA Ops:
  7.2 0.7 compare_reduce_fusion
  8.0 2.7 %copy_select_fusion.1 = (bf16[2,2,4,8,8,4,128]{6,5,2,4,1,3,0:T(4,128)(2,1)S(1)}, bf16[2,2,4,8,8,4,128]{6,5,2,4,1,3,0:T(4,128)(2,1)S(1)}) fusion(bf16[2,2,4,8,8,4,128]{6,4,5,3,2,1,0:T(8,128)(2,1)} %bitcast.98, pred[2,2,4]{2,1,0:T(4,128)(4,1)S(1)} %gt.24, bf16[2,2,4,8,8,4,128]{6,4,5,3,2,1,0:T(8,128)(2,1)} %bitcast.99), kind=kLoop, calls=%fused_computation.43 | loop fusion | flops 1048576 | bytes 4194320 | tf_op jit(solution)/shard_map/jit(_where)/select_n | solution.py:141
  10.7 1.3 collective-permute-start.1
  12.0 6.7 %collective-permute-start = (bf16[2,2,16,16,128]{4,3,2,1,0:T(8,128)(2,1)S(1)}, bf16[2,2,16,16,128]{4,3,2,1,0:T(8,128)(2,1)S(1)}, u32[]{:S(2)}, u32[]{:S(2)}) collective-permute-start(bf16[2,2,16,16,128]{4,3,2,1,0:T(8,128)(2,1)S(1)} %get-tuple-element.11), channel_id=1, source_target_pairs={{0,16},{4,20},{8,24},{12,28},{1,17},{5,21},{9,25},{13,29},{2,18},{... | collective-permute-start | bytes 786440 | tf_op jit(solution)/shard_map/ppermute | solution.py:18
  18.7 7.7 %all_gather.9 = bf16[27,64,64]{2,1,0:T(8,128)(2,1)S(1)} all-gather(bf16[27,16,64]{2,1,0:T(8,128)(2,1)S(1)} %copy-done.15), channel_id=1, replica_groups=mesh['space'=8,'fsdp'=4] {'fsdp'}, dimensions={1}, use_global_device_ids=true | all-gather | bytes 276480 | tf_op jit(solution)/shard_map/all_gather | solution.py:135
  26.4 1.7 collective-permute-done.1
  28.1 1.0 broadcast_select_fusion.5
  29.2 1.3 collective-permute-start.3
  30.6 4.8 %collective-permute-start.2 = (bf16[2,20,2,16,128]{4,3,2,1,0:T(8,128)(2,1)S(1)}, bf16[2,20,2,16,128]{4,3,2,1,0:T(8,128)(2,1)S(1)}, u32[]{:S(2)}, u32[]{:S(2)}) collective-permute-start(bf16[2,20,2,16,128]{4,3,2,1,0:T(8,128)(2,1)S(1)} %get-tuple-element.9), channel_id=1, source_target_pairs={{0,8},{4,12},{8,16},{12,20},{16,24},{20,28},{1,9},{5,13},{9,17},{1... | collective-permute-start | bytes 983048 | tf_op jit(solution)/shard_map/ppermute | solution.py:18
  35.7 5.6 %collective-permute-done.3 = bf16[2,20,2,16,128]{4,3,2,1,0:T(8,128)(2,1)S(1)} collective-permute-done((bf16[2,20,2,16,128]{4,3,2,1,0:T(8,128)(2,1)S(1)}, bf16[2,20,2,16,128]{4,3,2,1,0:T(8,128)(2,1)S(1)}, u32[]{:S(2)}, u32[]{:S(2)}) %collective-permute-start.3) | collective-permute-done | bytes 327712 | tf_op jit(solution)/shard_map/ppermute | solution.py:18
  41.3 1.2 collective-permute-done.2
  42.5 1.9 pad_maximum_fusion.7
  44.4 1.3 collective-permute-start.5
  45.7 0.5 convert_bitcast_fusion.1
  46.2 4.7 %collective-permute-start.4 = (bf16[2,20,20,1,128]{4,3,2,1,0:T(2,128)(2,1)S(1)}, bf16[2,20,20,1,128]{4,3,2,1,0:T(2,128)(2,1)S(1)}, u32[]{:S(2)}, u32[]{:S(2)}) collective-permute-start(bf16[2,20,20,1,128]{4,3,2,1,0:T(2,128)(2,1)S(1)} %get-tuple-element.7), channel_id=1, source_target_pairs={{0,4},{4,8},{8,12},{12,16},{16,20},{20,24},{24,28},{1,5},{5,9},{9,... | collective-permute-start | bytes 614408 | tf_op jit(solution)/shard_map/ppermute | solution.py:18
  50.9 6.3 %collective-permute-done.5 = bf16[2,20,20,1,128]{4,3,2,1,0:T(2,128)(2,1)S(1)} collective-permute-done((bf16[2,20,20,1,128]{4,3,2,1,0:T(2,128)(2,1)S(1)}, bf16[2,20,20,1,128]{4,3,2,1,0:T(2,128)(2,1)S(1)}, u32[]{:S(2)}, u32[]{:S(2)}) %collective-permute-start.5) | collective-permute-done | bytes 204832 | tf_op jit(solution)/shard_map/ppermute | solution.py:18
  57.3 0.4 broadcast_select_fusion.1
  57.7 8.5 %collective-permute-done.4 = bf16[2,20,20,1,128]{4,3,2,1,0:T(2,128)(2,1)S(1)} collective-permute-done((bf16[2,20,20,1,128]{4,3,2,1,0:T(2,128)(2,1)S(1)}, bf16[2,20,20,1,128]{4,3,2,1,0:T(2,128)(2,1)S(1)}, u32[]{:S(2)}, u32[]{:S(2)}) %collective-permute-start.4) | collective-permute-done | bytes 204832 | tf_op jit(solution)/shard_map/ppermute | solution.py:18
  66.6 5.9 %pad_maximum_fusion = bf16[2,20,20,18,128]{4,3,2,1,0:T(8,128)(2,1)S(1)} fusion(bf16[2,20,20,1,128]{4,3,2,1,0:T(2,128)(2,1)S(1)} %broadcast_select_fusion.1, bf16[2,20,2,16,128]{4,3,2,1,0:T(8,128)(2,1)S(1)} %broadcast_select_fusion.3, bf16[2,2,16,16,128]{4,3,2,1,0:T(8,128)(2,1)S(1)} %broadcast_select_fusion.5, bf16[1,16,16,16,128]{4,3,2,1,0:T(8,128)(2,1)S(1)} %bitcast.90, ...), kind=kLoop, calls=%fused_computation.6 | loop fusion | flops 29491200 | bytes 7372800 | tf_op jit(solution)/shard_map/concatenate | solution.py:63
  72.5 3.0 %fusion.29 = (bf16[20,20,20,128]{3,2,1,0:T(8,128)(2,1)}, bf16[20,20,1,20,128]{4,3,1,0,2:T(8,128)(2,1)S(1)}) fusion(bf16[2,20,20,18,128]{4,3,2,1,0:T(8,128)(2,1)S(1)} %pad_maximum_fusion), kind=kLoop, calls=%fused_computation.39 | loop fusion | bytes 7782400 | tf_op jit(solution)/shard_map/squeeze | solution.py:148
  75.8 0.7 pad.9.clone
  76.9 0.5 slice.93
  77.5 17.2 %add_multiply_fusion = (f32[18,18,8,3,128]{4,2,3,1,0:T(8,128)}, f32[18,18,8,3,128]{4,2,3,1,0:T(8,128)S(1)}) fusion(bf16[3,3,1,128,128]{4,3,2,1,0:T(8,128)(2,1)S(1)} %get-tuple-element.21, bf16[3,3,1,128,128]{4,3,2,1,0:T(8,128)(2,1)S(1)} %get-tuple-element.20, bf16[3,3,1,128,128]{4,3,2,1,0:T(8,128)(2,1)S(1)} %get-tuple-element.19, ...), kind=kOutput, calls=%fused_computation.17 | convolution fusion | flops 6900842496 | bytes 12738584 | tf_op jit(solution)/shard_map/conv_general_dilated | solution.py:102
  94.7 4.0 %copy.59 = f32[18,18,8,3,128]{4,3,2,1,0:T(4,128)} copy(f32[18,18,8,3,128]{4,2,3,1,0:T(8,128)S(1)} %get-tuple-element.27) | data formatting | bytes 7962624 | tf_op jit(solution)/shard_map/conv_general_dilated | solution.py:102
  98.6 7.3 %reshape.72 = f32[18,18,1,24,128]{4,3,1,0,2:T(8,128)} reshape(f32[18,18,8,3,128]{4,3,2,1,0:T(4,128)} %copy.59) | data formatting | bytes 7962624 | tf_op jit(solution)/shard_map/conv_general_dilated | solution.py:102
  105.9 4.5 %slice_bitcast_fusion.1 = f32[18,18,18,128]{3,2,1,0:T(8,128)} fusion(f32[18,18,1,24,128]{4,3,1,0,2:T(8,128)} %reshape.72), kind=kLoop, calls=%fused_computation.16 | loop fusion | bytes 5971968 | tf_op jit(solution)/shard_map/squeeze | solution.py:102
  110.5 3.0 %add_divide_fusion = f32[18,18,18,128]{3,2,1,0:T(8,128)} fusion(f32[18,18,1,24,128]{4,3,1,0,2:T(8,128)S(1)} %copy-done.1), kind=kLoop, calls=%fused_computation.18 | loop fusion | flops 2239488 | bytes 5971968 | tf_op jit(solution)/shard_map/div | solution.py:151
  113.5 3.9 %convert_bitcast_fusion = f32[18,18,18,128]{3,2,1,0:T(8,128)} fusion(bf16[2,20,20,18,128]{4,3,2,1,0:T(8,128)(2,1)} %copy-done), kind=kLoop, calls=%fused_computation.4 | loop fusion | flops 746496 | bytes 4478976 | tf_op jit(solution)/shard_map/convert_element_type | solution.py:153
  117.3 4.0 %copy.61 = f32[18,18,8,3,128]{4,3,2,1,0:T(4,128)} copy(f32[18,18,8,3,128]{4,2,3,1,0:T(8,128)S(1)} %copy-done.10) | data formatting | bytes 7962624 | tf_op jit(solution)/shard_map/mul | solution.py:152
  121.3 7.3 %reshape.81 = f32[18,18,1,24,128]{4,3,1,0,2:T(8,128)} reshape(f32[18,18,8,3,128]{4,3,2,1,0:T(4,128)} %copy.61) | data formatting | bytes 7962624 | tf_op jit(solution)/shard_map/mul | solution.py:152
  128.6 3.2 %fusion.22 = bf16[18,18,1,18,128]{4,3,1,0,2:T(8,128)(2,1)S(1)} fusion(f32[18,18,1,24,128]{4,3,1,0,2:T(8,128)} %reshape.81, bf16[2,20,20,18,128]{4,3,2,1,0:T(8,128)(2,1)} %copy-done), kind=kLoop, calls=%fused_computation.33 | loop fusion | flops 2239488 | bytes 5971968 | tf_op jit(solution)/shard_map/convert_element_type | solution.py:153
  132.1 2.9 %reshape.75 = bf16[18,18,1,8,3,128]{5,4,3,1,0,2:T(4,128)(2,1)} reshape(bf16[18,18,1,24,128]{4,3,1,0,2:T(8,128)(2,1)S(1)} %pad.11) | data formatting | bytes 3981312 | tf_op jit(solution)/shard_map/conv_general_dilated | solution.py:102
  135.1 2.2 copy.63
  137.4 1.5 slice.102
  138.9 1.1 slice_bitcast_fusion.2
  140.0 1.2 copy-done.2
  141.2 4.3 %fusion.31 = (bf16[1,16,16,16,128]{4,3,2,1,0:T(8,128)(2,1)S(1)}, f32[16,16,16,128]{3,2,1,0:T(8,128)}) fusion(f32[18,18,18,128]{3,2,1,0:T(8,128)S(1)} %copy-done.2, f32[18,18,18,128]{3,2,1,0:T(8,128)S(1)} %copy-done.3, f32[18,18,18,128]{3,2,1,0:T(8,128)} %convert_bitcast_fusion), kind=kLoop, calls=%fused_computation.41 | loop fusion | flops 3670016 | bytes 9437184 | tf_op jit(solution)/shard_map/broadcast_in_dim | solution.py:115
  145.5 32.2 %fusion.17 = f32[3,3,3,128,128]{4,3,2,1,0:T(8,128)S(1)} fusion(bf16[1,18,18,18,128]{4,3,2,1,0:T(8,128)(2,1)S(1)} %slice_bitcast_fusion.2, bf16[1,16,16,16,128]{4,3,2,1,0:T(8,128)(2,1)S(1)} %get-tuple-element.3), kind=kOutput, calls=%fused_computation.25 | convolution fusion | flops 3623878656 | bytes 4311040 | tf_op jit(solution)/shard_map/transpose | solution.py:121
  178.0 1.0 maximum_multiply_fusion
  179.1 0.5 copy-done.7
  179.9 13.6 %fusion.25 = f32[16,16,8,3,128]{4,2,3,1,0:T(8,128)S(1)} fusion(bf16[18,18,1,7,2,128]{5,3,4,1,0,2:T(8,128)(2,1)S(1)} %copy-done.11, bf16[18,18,1,8,3,128]{5,3,4,1,0,2:T(8,128)(2,1)S(1)} %copy-done.7, pred[8,3]{0,1:T(4,128)(4,1)S(1)} %copy-done.18, bf16[3,3,1,128,128]{4,3,2,1,0:T(8,128)(2,1)} %copy-done.14, bf16[3,3,1,128,128]{4,3,2,1,0:T(8,128)(2,1)} %copy-done.13, ...), kind=kOutput, calls=%fused_computation.37 | convolution fusion | flops 5447442432 | bytes 7182360 | tf_op jit(solution)/shard_map/conv_general_dilated | solution.py:102
  193.5 0.5 copy.64
  194.6 1.0 copy-done.4
  195.7 0.6 copy.60
  196.3 2.3 multiply_convert_fusion
  198.7 6.4 %reduce-scatter.2.cloned.1.call-done = f32[27,16,64]{2,1,0:T(8,128)} async-done(((f32[27,64,64]{2,1,0:T(8,128)}), f32[27,16,64]{2,1,0:T(8,128)}) %reduce-scatter.2.cloned.1.call-update) | async-done | bytes 110608 | tf_op jit(solution)/shard_map/reduce_scatter | solution.py:165
  205.0 39.5 %all-gather = f32[216,16,64]{2,1,0:T(8,128)S(1)} all-gather(f32[27,16,64]{2,1,0:T(8,128)} %reduce-scatter.2.cloned.1.call-done), channel_id=2, replica_groups=mesh['space'=8,'fsdp'=4] {'space'}, dimensions={0}, use_global_device_ids=true | all-gather | bytes 995328 | tf_op jit(solution)/shard_map/all_gather | solution.py:166
  244.5 0.8 reduce_sum.9
  (55 shorter events, 3.4 us)
Async XLA Ops:
  7.2 11.5 %copy-start.15 = (bf16[27,16,64]{2,1,0:T(8,128)(2,1)S(1)}, bf16[27,16,64]{2,1,0:T(8,128)(2,1)}, u32[]{:S(2)}) copy-start(bf16[27,16,64]{2,1,0:T(8,128)(2,1)} %param.7) | copy-start | bytes 165892
  7.2 197.9 %reduce-scatter.2.cloned.1.call-start = ((), (), s32[]{:S(2)}) async-start(), calls=%async_computation.1 | async-start | bytes 1105920 | tf_op jit(solution)/shard_map/reduce_scatter | solution.py:165
  10.7 17.4 %collective-permute-start.1 = (bf16[2,2,16,16,128]{4,3,2,1,0:T(8,128)(2,1)S(1)}, bf16[2,2,16,16,128]{4,3,2,1,0:T(8,128)(2,1)}, u32[]{:S(2)}, u32[]{:S(2)}) collective-permute-start(bf16[2,2,16,16,128]{4,3,2,1,0:T(8,128)(2,1)S(1)} %get-tuple-element.12), channel_id=1, source_target_pairs={{16,0},{20,4},{24,8},{28,12},{17,1},{21,5},{25,9},{29,13},{18,2},{... | collective-permute-start | bytes 786440 | tf_op jit(solution)/shard_map/ppermute | solution.py:18
  12.0 17.0 %collective-permute-start = (bf16[2,2,16,16,128]{4,3,2,1,0:T(8,128)(2,1)S(1)}, bf16[2,2,16,16,128]{4,3,2,1,0:T(8,128)(2,1)S(1)}, u32[]{:S(2)}, u32[]{:S(2)}) collective-permute-start(bf16[2,2,16,16,128]{4,3,2,1,0:T(8,128)(2,1)S(1)} %get-tuple-element.11), channel_id=1, source_target_pairs={{0,16},{4,20},{8,24},{12,28},{1,17},{5,21},{9,25},{13,29},{2,18},{... | collective-permute-start | bytes 786440 | tf_op jit(solution)/shard_map/ppermute | solution.py:18
  29.2 16.5 %copy-start.17 = (s32[1,16]{1,0:T(1,128)S(1)}, s32[1,16]{1,0:T(1,128)}, u32[]{:S(2)}) copy-start(s32[1,16]{1,0:T(1,128)} %param.6) | copy-start | bytes 196
  29.2 12.0 %collective-permute-start.3 = (bf16[2,20,2,16,128]{4,3,2,1,0:T(8,128)(2,1)S(1)}, bf16[2,20,2,16,128]{4,3,2,1,0:T(8,128)(2,1)S(1)}, u32[]{:S(2)}, u32[]{:S(2)}) collective-permute-start(bf16[2,20,2,16,128]{4,3,2,1,0:T(8,128)(2,1)S(1)} %get-tuple-element.10), channel_id=1, source_target_pairs={{8,0},{12,4},{16,8},{20,12},{24,16},{28,20},{9,1},{13,5},{17,9},{2... | collective-permute-start | bytes 983048 | tf_op jit(solution)/shard_map/ppermute | solution.py:18
  30.6 11.9 %collective-permute-start.2 = (bf16[2,20,2,16,128]{4,3,2,1,0:T(8,128)(2,1)S(1)}, bf16[2,20,2,16,128]{4,3,2,1,0:T(8,128)(2,1)S(1)}, u32[]{:S(2)}, u32[]{:S(2)}) collective-permute-start(bf16[2,20,2,16,128]{4,3,2,1,0:T(8,128)(2,1)S(1)} %get-tuple-element.9), channel_id=1, source_target_pairs={{0,8},{4,12},{8,16},{12,20},{16,24},{20,28},{1,9},{5,13},{9,17},{1... | collective-permute-start | bytes 983048 | tf_op jit(solution)/shard_map/ppermute | solution.py:18
  35.6 41.8 %copy-start.12 = (bf16[3,3,1,128,128]{4,3,2,1,0:T(8,128)(2,1)}, bf16[3,3,1,128,128]{4,3,2,1,0:T(8,128)(2,1)S(1)}, u32[]{:S(2)}) copy-start(bf16[3,3,1,128,128]{4,3,2,1,0:T(8,128)(2,1)S(1)} %get-tuple-element.19) | copy-start | bytes 884740
  35.6 41.8 %copy-start.13 = (bf16[3,3,1,128,128]{4,3,2,1,0:T(8,128)(2,1)}, bf16[3,3,1,128,128]{4,3,2,1,0:T(8,128)(2,1)S(1)}, u32[]{:S(2)}) copy-start(bf16[3,3,1,128,128]{4,3,2,1,0:T(8,128)(2,1)S(1)} %get-tuple-element.20) | copy-start | bytes 884740
  35.7 41.8 %copy-start.14 = (bf16[3,3,1,128,128]{4,3,2,1,0:T(8,128)(2,1)}, bf16[3,3,1,128,128]{4,3,2,1,0:T(8,128)(2,1)S(1)}, u32[]{:S(2)}) copy-start(bf16[3,3,1,128,128]{4,3,2,1,0:T(8,128)(2,1)S(1)} %get-tuple-element.21) | copy-start | bytes 884740
  44.4 12.9 %collective-permute-start.5 = (bf16[2,20,20,1,128]{4,3,2,1,0:T(2,128)(2,1)S(1)}, bf16[2,20,20,1,128]{4,3,2,1,0:T(2,128)(2,1)S(1)}, u32[]{:S(2)}, u32[]{:S(2)}) collective-permute-start(bf16[2,20,20,1,128]{4,3,2,1,0:T(2,128)(2,1)S(1)} %get-tuple-element.8), channel_id=1, source_target_pairs={{4,0},{8,4},{12,8},{16,12},{20,16},{24,20},{28,24},{5,1},{9,5},{13... | collective-permute-start | bytes 614408 | tf_op jit(solution)/shard_map/ppermute | solution.py:18
  46.2 20.0 %collective-permute-start.4 = (bf16[2,20,20,1,128]{4,3,2,1,0:T(2,128)(2,1)S(1)}, bf16[2,20,20,1,128]{4,3,2,1,0:T(2,128)(2,1)S(1)}, u32[]{:S(2)}, u32[]{:S(2)}) collective-permute-start(bf16[2,20,20,1,128]{4,3,2,1,0:T(2,128)(2,1)S(1)} %get-tuple-element.7), channel_id=1, source_target_pairs={{0,4},{4,8},{8,12},{12,16},{16,20},{20,24},{24,28},{1,5},{5,9},{9,... | collective-permute-start | bytes 614408 | tf_op jit(solution)/shard_map/ppermute | solution.py:18
  72.5 3.0 %copy-start = (bf16[2,20,20,18,128]{4,3,2,1,0:T(8,128)(2,1)}, bf16[2,20,20,18,128]{4,3,2,1,0:T(8,128)(2,1)S(1)}, u32[]{:S(2)}) copy-start(bf16[2,20,20,18,128]{4,3,2,1,0:T(8,128)(2,1)S(1)} %pad_maximum_fusion) | copy-start | bytes 11059204
  76.6 0.8 copy-start.19
  105.9 4.5 %copy-start.1 = (f32[18,18,1,24,128]{4,3,1,0,2:T(8,128)S(1)}, f32[18,18,1,24,128]{4,3,1,0,2:T(8,128)}, u32[]{:S(2)}) copy-start(f32[18,18,1,24,128]{4,3,1,0,2:T(8,128)} %reshape.72) | copy-start | bytes 11943940
  113.4 3.9 %copy-start.10 = (f32[18,18,8,3,128]{4,2,3,1,0:T(8,128)S(1)}, f32[18,18,8,3,128]{4,2,3,1,0:T(8,128)}, u32[]{:S(2)}) copy-start(f32[18,18,8,3,128]{4,2,3,1,0:T(8,128)} %get-tuple-element.26) | copy-start | bytes 11943940
  135.1 3.8 %copy-start.5 = (bf16[20,20,20,128]{3,2,1,0:T(8,128)(2,1)S(1)}, bf16[20,20,20,128]{3,2,1,0:T(8,128)(2,1)}, u32[]{:S(2)}) copy-start(bf16[20,20,20,128]{3,2,1,0:T(8,128)(2,1)} %get-tuple-element.5) | copy-start | bytes 6144004
  135.1 4.9 %copy-start.3 = (f32[18,18,18,128]{3,2,1,0:T(8,128)S(1)}, f32[18,18,18,128]{3,2,1,0:T(8,128)}, u32[]{:S(2)}) copy-start(f32[18,18,18,128]{3,2,1,0:T(8,128)} %add_divide_fusion) | copy-start | bytes 8957956
  137.3 8.1 %copy-start.6 = (bf16[18,18,1,8,3,128]{5,3,4,1,0,2:T(8,128)(2,1)}, bf16[18,18,1,8,3,128]{5,3,4,1,0,2:T(8,128)(2,1)S(1)}, u32[]{:S(2)}) copy-start(bf16[18,18,1,8,3,128]{5,3,4,1,0,2:T(8,128)(2,1)S(1)} %copy.63) | copy-start | bytes 5971972
  137.4 3.8 %copy-start.2 = (f32[18,18,18,128]{3,2,1,0:T(8,128)S(1)}, f32[18,18,18,128]{3,2,1,0:T(8,128)}, u32[]{:S(2)}) copy-start(f32[18,18,18,128]{3,2,1,0:T(8,128)} %slice_bitcast_fusion.1) | copy-start | bytes 8957956
  177.7 1.9 copy-start.7
  177.7 2.2 copy-start.11
  177.7 2.2 copy-start.18
  194.1 1.6 copy-start.4
  194.3 2.0 copy-start.8
  194.3 2.0 copy-start.9
  194.3 2.0 copy-start.16
Sparse Core Ops, SparseCore 0:
  179.2 25.7 reduce-scatter.1
